TPU v7x, 32 devices: a whole 2x2x4 slice. The times are simulated.
32 devices in a mesh: ctx: 8 (over y, x, core), uly: 4 (over z).
Axes of the slice: x: 2, y: 2, z: 4, core: 2. Of those that a mesh axis runs over, the one named last changes fastest.
Arguments:
- query_states: bfloat16 [1024, 2048], P(('ctx', 'uly')), may hold values from -8 to 8
- key_states: bfloat16 [1024, 2048], P(('ctx', 'uly')), may hold values from -8 to 8
- value_states: bfloat16 [1024, 2048], P(('ctx', 'uly')), may hold values from -6 to 6
- score_kernel: float32 [16, 6, 11], P('uly'), may hold values from -0.4 to 1.2
- head_mixing: float32 [16, 4], P('uly'), may hold values from 0.25 to 1
- head_gain: float32 [2048], P('uly'), may hold values from 0.5 to 1.5
Outputs:
- attended: bfloat16 [1024, 2048], P(('ctx', 'uly'))
All inputs are finite; a program needn't handle non-finite values.
Results may differ from a plain program's by a relative error of at most 0.0049.
Values may be sent and summed in bfloat16 or wider, within the bound.
No kernel may reach another device: no remote copies, remote signals or barrier semaphores. Data moves between devices by JAX's collectives and lax.ppermute only.
A program may use at most 64 MiB of HBM per device.

v0:
```python
import jax
import jax.numpy as jnp
from jax import lax
from jax.sharding import PartitionSpec as P

GROUP = 4
QCONV = 6
KCONV = 11
KEY_BLOCK = 128
ROW_CHUNK = 128
KEY_GROUP = 8
lowest = -1e30
epsilon = 1e-06


def passed_along(shard, axis, by):
    peers = lax.axis_size(axis)
    pairs = [(i, i + by) for i in range(peers) if 0 <= i + by < peers]
    return lax.ppermute(shard, axis, pairs)


def split_bf16(values):
    high = lax.reduce_precision(values, exponent_bits=8, mantissa_bits=7)
    low = values - high
    return (high.astype(jnp.bfloat16), low.astype(jnp.bfloat16))


def toeplitz_terms(score_kernel, head_dim):
    col_lead = KCONV - 1
    scaled = score_kernel * head_dim ** (-0.5)
    lag = (
        lax.iota(jnp.int32, KEY_BLOCK)[:, None]
        + col_lead
        - lax.iota(jnp.int32, KEY_BLOCK + col_lead)[None, :]
    )
    toeplitz = jnp.zeros(score_kernel.shape[:2] + lag.shape, jnp.float32)
    for col_lag in range(KCONV):
        toeplitz = jnp.where(lag == col_lag, scaled[:, :, col_lag, None, None], toeplitz)
    return split_bf16(toeplitz)


def convolved_keys(key_windows, terms):
    high, low = terms
    heads = high.shape[0]
    key_heads = key_windows.reshape(key_windows.shape[:2] + (heads, -1))
    conv_keys = jnp.einsum(
        "harc,nchd->nhard", high, key_heads, preferred_element_type=jnp.float32
    ) + jnp.einsum("harc,nchd->nhard", low, key_heads, preferred_element_type=jnp.float32)
    return split_bf16(conv_keys)


def band_terms(query_rows, query_first, key_flat, score_kernel):
    row_lead = QCONV - 1
    heads = score_kernel.shape[0]
    ext_count = query_rows.shape[0]
    row_count = ext_count - row_lead
    near = lax.dynamic_slice_in_dim(key_flat, query_first + 4, ext_count + QCONV - 2, 0)
    query_heads = query_rows.reshape(ext_count, heads, -1).astype(jnp.float32)
    near_heads = near.reshape(near.shape[0], heads, -1).astype(jnp.float32)
    scale = query_heads.shape[2] ** (-0.5)
    diagonals = [
        jnp.sum(query_heads * near_heads[lag - 1 : lag - 1 + ext_count], axis=2) * scale
        for lag in range(1, QCONV)
    ]
    band = []
    for gap in range(QCONV - 1):
        acc = jnp.zeros((row_count, heads), jnp.float32)
        for row_lag in range(gap + 1, QCONV):
            for col_lag in range(row_lag - gap):
                lag = row_lag - col_lag - gap
                acc = (
                    acc
                    - score_kernel[None, :, row_lag, col_lag]
                    * diagonals[lag - 1][row_lead - row_lag : row_lead - row_lag + row_count]
                )
        band.append(acc.T)
    return jnp.stack(band)


def group_logits(shifted, key_windows, terms):
    keys_high, keys_low = convolved_keys(key_windows, terms)
    return jnp.einsum(
        "ihad,nhard->hinr", shifted, keys_high, preferred_element_type=jnp.float32
    ) + jnp.einsum("ihad,nhard->hinr", shifted, keys_low, preferred_element_type=jnp.float32)


def attend_chunk(shifted, band, query_first, key_windows, terms, value_heads, head_mixing):
    row_count, heads = shifted.shape[:2]
    seq_len = value_heads.shape[0]
    window_count = key_windows.shape[0]
    if window_count <= KEY_GROUP:
        convolved = group_logits(shifted, key_windows, terms)
    else:
        grouped_windows = key_windows.reshape(
            (window_count // KEY_GROUP, KEY_GROUP) + key_windows.shape[1:]
        )
        convolved = lax.map(lambda windows: group_logits(shifted, windows, terms), grouped_windows)
        convolved = jnp.moveaxis(convolved, 0, 2)
    convolved = convolved.reshape(heads, row_count, seq_len)
    query_pos = query_first + lax.iota(jnp.int32, row_count)
    gap = query_pos[:, None] - lax.iota(jnp.int32, seq_len)[None, :]
    for lag in range(QCONV - 1):
        convolved = convolved + jnp.where(gap == lag, band[lag][:, :, None], 0.0)
    logits = jnp.where(gap >= 0, convolved, lowest)
    peak = jnp.max(logits, axis=2, keepdims=True)
    expd = jnp.exp(logits - peak)
    probabilities = expd / jnp.sum(expd, axis=2, keepdims=True)
    grouped = probabilities.reshape(heads // GROUP, GROUP, row_count, seq_len)
    weights = head_mixing.reshape(heads // GROUP, GROUP, GROUP)
    mixed_probs = jnp.zeros_like(grouped)
    for source in range(GROUP):
        mixed_probs = mixed_probs + weights[:, :, source, None, None] * grouped[:, source, None]
    mixed_probs = mixed_probs.reshape(heads, row_count, seq_len).astype(jnp.bfloat16)
    return jnp.einsum("hik,khd->ihd", mixed_probs, value_heads, preferred_element_type=jnp.float32)


def normalize(weighted, gain_local):
    factor = lax.rsqrt(jnp.mean(weighted * weighted, axis=2, keepdims=True) + epsilon)
    return (
        (weighted * factor * gain_local[None]).astype(jnp.bfloat16).reshape(weighted.shape[0], -1)
    )


def shards(query_states, key_states, value_states, score_kernel, head_mixing, head_gain):
    stacked = jnp.stack([query_states, key_states, value_states])
    query_local, key_local, value_local = lax.all_to_all(
        stacked, "uly", split_axis=2, concat_axis=1, tiled=True
    )
    shard_rows = query_local.shape[0]
    width = query_local.shape[1]
    row_lead = QCONV - 1
    col_lead = KCONV - 1
    heads = score_kernel.shape[0]
    head_dim = width // heads
    ctx_place = lax.axis_index("ctx")
    query_first = ctx_place * shard_rows
    earlier = passed_along(query_local[shard_rows - row_lead :], "ctx", 1)
    query_ext = jnp.concatenate([earlier, query_local], axis=0)
    key_all, value_all = lax.all_gather(
        jnp.stack([key_local, value_local]), "ctx", axis=1, tiled=True
    )
    seq_len = key_all.shape[0]
    key_pad = jnp.concatenate([jnp.zeros((col_lead, width), key_all.dtype), key_all], axis=0)
    key_windows = jnp.stack(
        [key_pad[start : start + KEY_BLOCK + col_lead] for start in range(0, seq_len, KEY_BLOCK)]
    )
    terms = toeplitz_terms(score_kernel, head_dim)
    edge = jnp.zeros((8, width), key_all.dtype)
    key_flat = jnp.concatenate([edge, key_all, edge], axis=0)
    band = band_terms(query_ext, query_first, key_flat, score_kernel)
    query_heads = query_ext.reshape(shard_rows + row_lead, heads, head_dim)
    shifted = jnp.stack(
        [query_heads[row_lead - lag : row_lead - lag + shard_rows] for lag in range(QCONV)], axis=2
    )
    value_heads = value_all.reshape(seq_len, heads, head_dim)
    chunk = min(ROW_CHUNK * KEY_BLOCK * 8 // seq_len, shard_rows)
    if chunk == shard_rows:
        weighted = attend_chunk(
            shifted, band, query_first, key_windows, terms, value_heads, head_mixing
        )
    else:
        chunks = shard_rows // chunk

        def one_chunk(index):
            start = index * chunk
            return attend_chunk(
                lax.dynamic_slice_in_dim(shifted, start, chunk, 0),
                lax.dynamic_slice_in_dim(band, start, chunk, 2),
                query_first + start,
                key_windows,
                terms,
                value_heads,
                head_mixing,
            )

        weighted = lax.map(one_chunk, jnp.arange(chunks, dtype=jnp.int32))
        weighted = weighted.reshape((shard_rows,) + weighted.shape[2:])
    gain_local = head_gain.reshape(heads, head_dim)
    attended = normalize(weighted, gain_local)
    return lax.all_to_all(attended, "uly", split_axis=0, concat_axis=1, tiled=True)


def solution(mesh):
    placed = (
        P(("ctx", "uly"), None),
        P(("ctx", "uly"), None),
        P(("ctx", "uly"), None),
        P("uly", None, None),
        P("uly", None),
        P("uly"),
    )
    return jax.shard_map(
        shards, mesh=mesh, in_specs=placed, out_specs=P(("ctx", "uly"), None), check_vma=False
    )
```

profile of v0, /device:TPU:0, one launch (start us, length us, event | category | flops | bytes accessed | tf_op | source)
XLA Modules:
  0.0 156.9 jit_solution(3671239521716522393)
XLA Ops:
  6.5 1.1 pad_maximum_fusion
  7.6 1.4 copy.223
  9.0 1.6 %reshape.295 = bf16[4,2,24576]{2,1,0:T(2,128)(2,1)S(1)} reshape(bf16[2048,3,32]{2,1,0:T(4,128)(2,1)S(1)} %bitcast.118) | data formatting | bytes 786432
  10.6 17.8 %all_to_all.34 = bf16[4,2,24576]{2,1,0:T(2,128)(2,1)S(1)} all-to-all(bf16[4,2,24576]{2,1,0:T(2,128)(2,1)S(1)} %reshape.295), channel_id=1, replica_groups=mesh['ctx'=8,'uly'=4] {'uly'}, dimensions={0} | all-to-all | bytes 786432 | tf_op jit(solution)/shard_map/all_to_all | solution.py:126
  28.4 1.3 reshape.296
  29.7 1.2 copy.282
  30.9 0.1 fusion.128
  31.1 0.8 pad_maximum_fusion.1
  32.5 0.7 copy.255
  33.2 0.6 copy.254
  33.8 0.7 copy.253
  34.5 0.7 copy.252
  35.2 0.7 copy.251
  35.9 0.7 copy.250
  36.5 0.7 copy.249
  37.2 0.7 slice_reduce_fusion.18
  38.0 1.0 slice_reduce_fusion.17
  39.0 0.8 fusion.108
  39.7 1.2 fusion.84
  41.0 1.2 subtract_compare_fusion.5
  42.3 1.3 collective-permute-start
  43.6 0.7 concatenate.20
  45.2 0.1 copy.238
  45.7 0.1 copy.240
  45.8 0.6 concatenate.19
  46.6 12.5 %all-gather.2.cloned.1.call-done = bf16[2,1024,512]{2,1,0:T(8,128)(2,1)} async-done(((bf16[2,128,512]{2,1,0:T(8,128)(2,1)}), bf16[2,1024,512]{2,1,0:T(8,128)(2,1)}) %all-gather.2.cloned.1.call-update) | async-done | bytes 2097168 | tf_op jit(solution)/shard_map/all_gather | solution.py:139
  59.1 1.7 %slice_bitcast_fusion = (bf16[1024,512]{1,0:T(8,128)(2,1)S(1)}, bf16[1,1024,512]{2,1,0:T(8,128)(2,1)S(1)}) fusion(bf16[2,1024,512]{2,1,0:T(8,128)(2,1)} %all-gather.2.cloned.1.call-done), kind=kLoop, calls=%fused_computation.39 | loop fusion | bytes 4194304 | tf_op jit(solution)/shard_map/unstack | solution.py:139
  60.8 0.7 pad_slice_fusion
  61.5 1.6 %stack.75 = bf16[1,138,4,128]{3,2,1,0:T(4,128)(2,1)} reshape(bf16[138,512]{1,0:T(8,128)(2,1)} %pad_slice_fusion) | data formatting | bytes 282624 | tf_op jit(solution)/shard_map/stack | solution.py:144
  63.1 1.6 %copy_dynamic-update-slice_fusion.7 = bf16[8,138,4,128]{3,1,0,2:T(8,128)(2,1)} fusion(bf16[1,138,4,128]{3,2,1,0:T(4,128)(2,1)} %stack.75), kind=kLoop, calls=%fused_computation.138 | loop fusion | bytes 288768
  64.7 2.4 %fusion.127 = (bf16[1,138,512]{2,1,0:T(8,128)(2,1)}, bf16[1,138,512]{2,1,0:T(8,128)(2,1)}, bf16[1,138,512]{2,1,0:T(8,128)(2,1)}, bf16[1,138,512]{2,1,0:T(8,128)(...) fusion(bf16[2,1024,512]{2,1,0:T(8,128)(2,1)} %all-gather.2.cloned.1.call-done), kind=kLoop, calls=%fused_computation.217 | loop fusion | bytes 1978368 | tf_op jit(solution)/shard_map/slice | solution.py:145
  67.1 1.6 %stack.76 = bf16[1,138,4,128]{3,2,1,0:T(4,128)(2,1)} reshape(bf16[1,138,512]{2,1,0:T(8,128)(2,1)} %get-tuple-element.39) | data formatting | bytes 282624 | tf_op jit(solution)/shard_map/stack | solution.py:144
  68.7 1.6 %stack.77 = bf16[1,138,4,128]{3,2,1,0:T(4,128)(2,1)} reshape(bf16[1,138,512]{2,1,0:T(8,128)(2,1)} %get-tuple-element.38) | data formatting | bytes 282624 | tf_op jit(solution)/shard_map/stack | solution.py:144
  70.3 1.6 %stack.78 = bf16[1,138,4,128]{3,2,1,0:T(4,128)(2,1)} reshape(bf16[1,138,512]{2,1,0:T(8,128)(2,1)} %get-tuple-element.37) | data formatting | bytes 282624 | tf_op jit(solution)/shard_map/stack | solution.py:144
  71.9 1.6 %stack.79 = bf16[1,138,4,128]{3,2,1,0:T(4,128)(2,1)} reshape(bf16[1,138,512]{2,1,0:T(8,128)(2,1)} %get-tuple-element.36) | data formatting | bytes 282624 | tf_op jit(solution)/shard_map/stack | solution.py:144
  73.5 1.6 %stack.80 = bf16[1,138,4,128]{3,2,1,0:T(4,128)(2,1)} reshape(bf16[1,138,512]{2,1,0:T(8,128)(2,1)} %get-tuple-element.35) | data formatting | bytes 282624 | tf_op jit(solution)/shard_map/stack | solution.py:144
  75.1 1.6 %stack.81 = bf16[1,138,4,128]{3,2,1,0:T(4,128)(2,1)} reshape(bf16[1,138,512]{2,1,0:T(8,128)(2,1)} %get-tuple-element.34) | data formatting | bytes 282624 | tf_op jit(solution)/shard_map/stack | solution.py:144
  76.7 1.6 %stack.82 = bf16[1,138,4,128]{3,2,1,0:T(4,128)(2,1)} reshape(bf16[1,138,512]{2,1,0:T(8,128)(2,1)} %get-tuple-element.33) | data formatting | bytes 282624 | tf_op jit(solution)/shard_map/stack | solution.py:144
  78.3 1.6 %copy_dynamic-update-slice_fusion.6 = bf16[8,138,4,128]{3,1,0,2:T(8,128)(2,1)} fusion(bf16[8,138,4,128]{3,1,0,2:T(8,128)(2,1)} %copy_dynamic-update-slice_fusion.7, bf16[1,138,4,128]{3,2,1,0:T(4,128)(2,1)} %stack.76), kind=kLoop, calls=%fused_computation.137 | loop fusion | bytes 288768
  79.9 1.6 %copy_dynamic-update-slice_fusion.5 = bf16[8,138,4,128]{3,1,0,2:T(8,128)(2,1)} fusion(bf16[8,138,4,128]{3,1,0,2:T(8,128)(2,1)} %copy_dynamic-update-slice_fusion.6, bf16[1,138,4,128]{3,2,1,0:T(4,128)(2,1)} %stack.77), kind=kLoop, calls=%fused_computation.136 | loop fusion | bytes 288768
  81.5 1.6 %copy_dynamic-update-slice_fusion.4 = bf16[8,138,4,128]{3,1,0,2:T(8,128)(2,1)} fusion(bf16[8,138,4,128]{3,1,0,2:T(8,128)(2,1)} %copy_dynamic-update-slice_fusion.5, bf16[1,138,4,128]{3,2,1,0:T(4,128)(2,1)} %stack.78), kind=kLoop, calls=%fused_computation.135 | loop fusion | bytes 288768
  83.1 1.6 %copy_dynamic-update-slice_fusion.3 = bf16[8,138,4,128]{3,1,0,2:T(8,128)(2,1)} fusion(bf16[8,138,4,128]{3,1,0,2:T(8,128)(2,1)} %copy_dynamic-update-slice_fusion.4, bf16[1,138,4,128]{3,2,1,0:T(4,128)(2,1)} %stack.79), kind=kLoop, calls=%fused_computation.134 | loop fusion | bytes 288768
  84.7 1.6 %copy_dynamic-update-slice_fusion.2 = bf16[8,138,4,128]{3,1,0,2:T(8,128)(2,1)} fusion(bf16[8,138,4,128]{3,1,0,2:T(8,128)(2,1)} %copy_dynamic-update-slice_fusion.3, bf16[1,138,4,128]{3,2,1,0:T(4,128)(2,1)} %stack.80), kind=kLoop, calls=%fused_computation.133 | loop fusion | bytes 288768
  86.3 1.6 %copy_dynamic-update-slice_fusion.1 = bf16[8,138,4,128]{3,1,0,2:T(8,128)(2,1)} fusion(bf16[8,138,4,128]{3,1,0,2:T(8,128)(2,1)} %copy_dynamic-update-slice_fusion.2, bf16[1,138,4,128]{3,2,1,0:T(4,128)(2,1)} %stack.81), kind=kLoop, calls=%fused_computation.132 | loop fusion | bytes 288768
  87.9 1.6 %copy_dynamic-update-slice_fusion = bf16[8,138,4,128]{3,1,0,2:T(8,128)(2,1)} fusion(bf16[8,138,4,128]{3,1,0,2:T(8,128)(2,1)} %copy_dynamic-update-slice_fusion.1, bf16[1,138,4,128]{3,2,1,0:T(4,128)(2,1)} %stack.82), kind=kLoop, calls=%fused_computation.131 | loop fusion | bytes 288768 | tf_op jit(solution)/shard_map/stack | solution.py:144
  89.6 8.7 %fusion.17 = f32[4,8,128,6,128]{4,2,3,1,0:T(8,128)} fusion(bf16[8,138,4,128]{3,1,0,2:T(8,128)(2,1)} %copy_dynamic-update-slice_fusion, f32[4,6]{1,0:T(4,128)S(1)} %bitcast.135, f32[4,6]{1,0:T(4,128)S(1)} %bitcast.137, f32[4,6]{1,0:T(4,128)S(1)} %bitcast.139, f32[4,6]{1,0:T(4,128)S(1)} %bitcast.141, f32[4,6]{1,0:T(4,128)} %bitcast.143, ...), kind=kOutput, calls=%fused_computation.32 | convolution fusion | flops 873732096 | bytes 13908768 | tf_op jit(solution)/shard_map/harc,nchd->nhard/dot_general | solution.py:46
  98.5 6.3 %fusion.15 = f32[4,8,128,6,128]{4,2,3,1,0:T(8,128)} fusion(bf16[8,138,4,128]{3,1,0,2:T(8,128)(2,1)S(1)} %copy-done, f32[4,6]{1,0:T(4,128)S(1)} %bitcast.136, f32[4,6]{1,0:T(4,128)S(1)} %bitcast.138, f32[4,6]{1,0:T(4,128)S(1)} %bitcast.140, f32[4,6]{1,0:T(4,128)S(1)} %bitcast.142, f32[4,6]{1,0:T(4,128)S(1)} %bitcast.144, f32[4,6]{1,0:T(4,128)S(1)} %bitcast.146, ...), kind=kOutput, calls=%fused_computation.30 | convolution fusion | flops 874156032 | bytes 13908768 | tf_op jit(solution)/shard_map/harc,nchd->nhard/dot_general | solution.py:48
  104.8 1.4 copy.227
  106.3 0.1 fusion.129
  107.0 0.2 copy-done.5
  107.2 0.8 fusion.90
  108.6 10.9 %fusion.1 = f32[4,128,8,128,1]{1,3,4,2,0:T(8,128)S(1)} fusion(f32[4,8,128,6,128]{4,2,3,1,0:T(8,128)} %fusion.17, f32[4,8,128,6,128]{4,2,3,1,0:T(8,128)} %fusion.15, bf16[128,4,6,128]{3,0,2,1:T(8,128)(2,1)S(1)} %constant_dynamic-update-slice_fusion), kind=kOutput, calls=%fused_computation.3 | convolution fusion | flops 817889280 | bytes 28049408 | tf_op jit(solution)/shard_map/ihad,nhard->hinr/dot_general | solution.py:84
  119.9 10.4 %fusion.85 = (f32[4,128]{1,0:T(4,128)S(1)}, f32[4,128,8,128]{1,3,2,0:T(8,128)S(1)}) fusion(f32[4,128]{1,0:T(4,128)S(1)} %get-tuple-element.74, pred[128,8,128]{0,2,1:T(8,128)(4,1)S(1)} %get-tuple-element.69, f32[4,128]{1,0:T(4,128)S(1)} %get-tuple-element.67, pred[128,8,128]{0,2,1:T(8,128)(4,1)S(1)} %get-tuple-element.70, ...), kind=kOutput, calls=%fused_computation.115 | convolution fusion | flops 821558784 | bytes 30945280 | tf_op jit(solution)/shard_map/ihad,nhard->hinr/dot_general | solution.py:82
  130.4 1.3 exponential_reduce_fusion
  131.7 1.3 fusion.13
  133.0 0.1 slice_bitcast_fusion.4
  133.1 1.0 copy.271
  134.1 1.0 copy.270
  135.2 1.0 copy.269
  136.2 0.2 copy.268
  136.5 1.8 %multiply_reduce_fusion = (f32[128,4]{0,1:T(4,128)S(1)}, f32[128,4,128]{0,2,1:T(8,128)S(1)}) fusion(bf16[1024,4,128]{0,2,1:T(8,128)(2,1)S(1)} %bitcast.123, f32[128,1024]{1,0:T(8,128)S(1)} %copy-done.3, f32[4]{0:T(128)S(1)} %copy-done.50, f32[128,1024]{1,0:T(8,128)S(1)} %copy-done.4, f32[4]{0:T(128)S(1)} %copy-done.51, f32[128,1024]{1,0:T(8,128)} %copy.269, ...), kind=kOutput, calls=%fused_computation.127 | convolution fusion | flops 138542592 | bytes 3409984 | tf_op jit(solution)/shard_map/hik,khd->ihd/dot_general | solution.py:114
  138.5 0.1 copy.272
  138.7 10.7 %all_to_all.35 = bf16[4,32,512]{2,1,0:T(8,128)(2,1)S(1)} all-to-all(bf16[4,32,512]{2,1,0:T(8,128)(2,1)S(1)} %all_to_all.28), channel_id=1, replica_groups=mesh['ctx'=8,'uly'=4] {'uly'}, dimensions={0} | all-to-all | bytes 262144 | tf_op jit(solution)/shard_map/all_to_all | solution.py:180
  149.4 0.7 copy.284
  (158 shorter events, 3.8 us)
Async XLA Ops:
  6.5 52.5 %all-gather.2.cloned.1.call-start = ((), (), s32[]{:S(2)}) async-start(), calls=%async_computation.2 | async-start | bytes 2359296 | tf_op jit(solution)/shard_map/all_gather | solution.py:139
  29.7 2.2 %copy-start.23 = (f32[4,6,11]{2,0,1:T(4,128)S(1)}, f32[4,6,11]{2,0,1:T(4,128)}, u32[]{:S(2)}) copy-start(f32[4,6,11]{2,0,1:T(4,128)} %param.9) | copy-start | bytes 3172
  29.7 7.5 %copy-start.31 = (f32[4,4]{1,0:T(4,128)S(1)}, f32[4,4]{1,0:T(4,128)}, u32[]{:S(2)}) copy-start(f32[4,4]{1,0:T(4,128)} %param.10) | copy-start | bytes 196
  42.3 2.1 %collective-permute-start = (bf16[5,512]{1,0:T(8,128)(2,1)S(1)}, bf16[5,512]{1,0:T(8,128)(2,1)S(1)}, u32[]{:S(2)}, u32[]{:S(2)}) collective-permute-start(bf16[5,512]{1,0:T(8,128)(2,1)S(1)} %slice.356), channel_id=1, source_target_pairs={{0,4},{4,8},{8,12},{12,16},{16,20},{20,24},{24,28},{1,5},{5,9},{9,... | collective-permute-start | bytes 15368 | tf_op jit(solution)/shard_map/ppermute | solution.py:19
  89.5 8.9 %copy-start = (bf16[8,138,4,128]{3,1,0,2:T(8,128)(2,1)S(1)}, bf16[8,138,4,128]{3,1,0,2:T(8,128)(2,1)}, u32[]{:S(2)}) copy-start(bf16[8,138,4,128]{3,1,0,2:T(8,128)(2,1)} %copy_dynamic-update-slice_fusion) | copy-start | bytes 3391492
  89.5 8.9 %copy-start.12 = (pred[128,138]{0,1:T(8,128)(4,1)S(1)}, pred[128,138]{0,1:T(8,128)(4,1)}, u32[]{:S(2)}) copy-start(pred[128,138]{0,1:T(8,128)(4,1)} %get-tuple-element.81) | copy-start | bytes 52996
  89.5 8.9 %copy-start.13 = (pred[128,138]{0,1:T(8,128)(4,1)S(1)}, pred[128,138]{0,1:T(8,128)(4,1)}, u32[]{:S(2)}) copy-start(pred[128,138]{0,1:T(8,128)(4,1)} %get-tuple-element.82) | copy-start | bytes 52996
  89.5 8.9 %copy-start.14 = (pred[128,138]{0,1:T(8,128)(4,1)S(1)}, pred[128,138]{0,1:T(8,128)(4,1)}, u32[]{:S(2)}) copy-start(pred[128,138]{0,1:T(8,128)(4,1)} %get-tuple-element.83) | copy-start | bytes 52996
  89.5 8.9 %copy-start.15 = (pred[128,138]{0,1:T(8,128)(4,1)S(1)}, pred[128,138]{0,1:T(8,128)(4,1)}, u32[]{:S(2)}) copy-start(pred[128,138]{0,1:T(8,128)(4,1)} %get-tuple-element.84) | copy-start | bytes 52996
  89.5 8.9 %copy-start.16 = (pred[128,138]{0,1:T(8,128)(4,1)S(1)}, pred[128,138]{0,1:T(8,128)(4,1)}, u32[]{:S(2)}) copy-start(pred[128,138]{0,1:T(8,128)(4,1)} %get-tuple-element.85) | copy-start | bytes 52996
  89.5 8.9 %copy-start.17 = (pred[128,138]{0,1:T(8,128)(4,1)S(1)}, pred[128,138]{0,1:T(8,128)(4,1)}, u32[]{:S(2)}) copy-start(pred[128,138]{0,1:T(8,128)(4,1)} %get-tuple-element.86) | copy-start | bytes 52996
  89.5 8.9 %copy-start.18 = (pred[128,138]{0,1:T(8,128)(4,1)S(1)}, pred[128,138]{0,1:T(8,128)(4,1)}, u32[]{:S(2)}) copy-start(pred[128,138]{0,1:T(8,128)(4,1)} %get-tuple-element.87) | copy-start | bytes 52996
  89.5 8.9 %copy-start.19 = (pred[128,138]{0,1:T(8,128)(4,1)S(1)}, pred[128,138]{0,1:T(8,128)(4,1)}, u32[]{:S(2)}) copy-start(pred[128,138]{0,1:T(8,128)(4,1)} %get-tuple-element.88) | copy-start | bytes 52996
  89.5 8.9 %copy-start.20 = (pred[128,138]{0,1:T(8,128)(4,1)S(1)}, pred[128,138]{0,1:T(8,128)(4,1)}, u32[]{:S(2)}) copy-start(pred[128,138]{0,1:T(8,128)(4,1)} %get-tuple-element.89) | copy-start | bytes 52996
  89.5 8.9 %copy-start.21 = (pred[128,138]{0,1:T(8,128)(4,1)S(1)}, pred[128,138]{0,1:T(8,128)(4,1)}, u32[]{:S(2)}) copy-start(pred[128,138]{0,1:T(8,128)(4,1)} %get-tuple-element.90) | copy-start | bytes 52996
  89.6 8.9 %copy-start.22 = (pred[128,138]{0,1:T(8,128)(4,1)S(1)}, pred[128,138]{0,1:T(8,128)(4,1)}, u32[]{:S(2)}) copy-start(pred[128,138]{0,1:T(8,128)(4,1)} %get-tuple-element.91) | copy-start | bytes 52996
  89.6 8.9 %copy-start.24 = (f32[4,6,1]{1,0,2:T(4,128)S(1)}, f32[4,6,1]{1,0,2:T(4,128)}, u32[]{:S(2)}) copy-start(f32[4,6,1]{1,0,2:T(4,128)} %copy.255) | copy-start | bytes 292
  89.6 8.9 %copy-start.25 = (f32[4,6,1]{1,0,2:T(4,128)S(1)}, f32[4,6,1]{1,0,2:T(4,128)}, u32[]{:S(2)}) copy-start(f32[4,6,1]{1,0,2:T(4,128)} %copy.254) | copy-start | bytes 292
  89.6 8.9 %copy-start.26 = (f32[4,6,1]{1,0,2:T(4,128)S(1)}, f32[4,6,1]{1,0,2:T(4,128)}, u32[]{:S(2)}) copy-start(f32[4,6,1]{1,0,2:T(4,128)} %copy.253) | copy-start | bytes 292
  89.6 8.9 %copy-start.27 = (f32[4,6,1]{1,0,2:T(4,128)S(1)}, f32[4,6,1]{1,0,2:T(4,128)}, u32[]{:S(2)}) copy-start(f32[4,6,1]{1,0,2:T(4,128)} %copy.252) | copy-start | bytes 292
  89.6 8.9 %copy-start.28 = (f32[4,6,1]{1,0,2:T(4,128)S(1)}, f32[4,6,1]{1,0,2:T(4,128)}, u32[]{:S(2)}) copy-start(f32[4,6,1]{1,0,2:T(4,128)} %copy.251) | copy-start | bytes 292
  89.6 8.9 %copy-start.29 = (f32[4,6,1]{1,0,2:T(4,128)S(1)}, f32[4,6,1]{1,0,2:T(4,128)}, u32[]{:S(2)}) copy-start(f32[4,6,1]{1,0,2:T(4,128)} %copy.250) | copy-start | bytes 292
  89.6 8.9 %copy-start.30 = (f32[4,6,1]{1,0,2:T(4,128)S(1)}, f32[4,6,1]{1,0,2:T(4,128)}, u32[]{:S(2)}) copy-start(f32[4,6,1]{1,0,2:T(4,128)} %copy.249) | copy-start | bytes 292
  106.3 0.9 copy-start.5
  106.3 0.9 copy-start.32
  108.4 11.0 %copy-start.33 = (f32[4]{0:T(128)S(1)}, f32[4]{0:T(128)}, u32[]{:S(2)}) copy-start(f32[4]{0:T(128)} %get-tuple-element.11) | copy-start | bytes 52
  108.4 11.0 %copy-start.34 = (f32[4]{0:T(128)S(1)}, f32[4]{0:T(128)}, u32[]{:S(2)}) copy-start(f32[4]{0:T(128)} %get-tuple-element.12) | copy-start | bytes 52
  108.4 11.0 %copy-start.35 = (f32[4]{0:T(128)S(1)}, f32[4]{0:T(128)}, u32[]{:S(2)}) copy-start(f32[4]{0:T(128)} %get-tuple-element.13) | copy-start | bytes 52
  108.5 11.0 %copy-start.36 = (f32[4]{0:T(128)S(1)}, f32[4]{0:T(128)}, u32[]{:S(2)}) copy-start(f32[4]{0:T(128)} %get-tuple-element.16) | copy-start | bytes 52
  108.5 11.0 %copy-start.37 = (f32[4]{0:T(128)S(1)}, f32[4]{0:T(128)}, u32[]{:S(2)}) copy-start(f32[4]{0:T(128)} %get-tuple-element.17) | copy-start | bytes 52
  108.5 11.0 %copy-start.38 = (f32[4]{0:T(128)S(1)}, f32[4]{0:T(128)}, u32[]{:S(2)}) copy-start(f32[4]{0:T(128)} %get-tuple-element.20) | copy-start | bytes 52
  108.5 11.1 %copy-start.39 = (f32[4]{0:T(128)S(1)}, f32[4]{0:T(128)}, u32[]{:S(2)}) copy-start(f32[4]{0:T(128)} %get-tuple-element.15) | copy-start | bytes 52
  108.5 11.1 %copy-start.40 = (f32[4]{0:T(128)S(1)}, f32[4]{0:T(128)}, u32[]{:S(2)}) copy-start(f32[4]{0:T(128)} %get-tuple-element.19) | copy-start | bytes 52
  108.5 11.1 %copy-start.41 = (f32[4]{0:T(128)S(1)}, f32[4]{0:T(128)}, u32[]{:S(2)}) copy-start(f32[4]{0:T(128)} %get-tuple-element.22) | copy-start | bytes 52
  108.5 11.1 %copy-start.42 = (f32[4]{0:T(128)S(1)}, f32[4]{0:T(128)}, u32[]{:S(2)}) copy-start(f32[4]{0:T(128)} %get-tuple-element.24) | copy-start | bytes 52
  108.5 11.2 %copy-start.44 = (f32[4]{0:T(128)S(1)}, f32[4]{0:T(128)}, u32[]{:S(2)}) copy-start(f32[4]{0:T(128)} %get-tuple-element.10) | copy-start | bytes 52
  108.5 11.2 %copy-start.45 = (f32[4]{0:T(128)S(1)}, f32[4]{0:T(128)}, u32[]{:S(2)}) copy-start(f32[4]{0:T(128)} %get-tuple-element.14) | copy-start | bytes 52
  108.5 11.2 %copy-start.46 = (f32[4]{0:T(128)S(1)}, f32[4]{0:T(128)}, u32[]{:S(2)}) copy-start(f32[4]{0:T(128)} %get-tuple-element.18) | copy-start | bytes 52
  108.6 11.2 %copy-start.47 = (f32[4]{0:T(128)S(1)}, f32[4]{0:T(128)}, u32[]{:S(2)}) copy-start(f32[4]{0:T(128)} %get-tuple-element.21) | copy-start | bytes 52
  108.6 11.2 %copy-start.48 = (f32[4]{0:T(128)S(1)}, f32[4]{0:T(128)}, u32[]{:S(2)}) copy-start(f32[4]{0:T(128)} %get-tuple-element.23) | copy-start | bytes 52
  108.6 11.3 %copy-start.1 = (pred[128,8,128]{0,2,1:T(8,128)(4,1)S(1)}, pred[128,8,128]{0,2,1:T(8,128)(4,1)}, u32[]{:S(2)}) copy-start(pred[128,8,128]{0,2,1:T(8,128)(4,1)} %get-tuple-element.73) | copy-start | bytes 393220
  130.3 1.3 copy-start.6
  130.3 1.3 copy-start.7
  130.3 1.3 copy-start.8
  130.4 1.3 copy-start.9
  130.4 1.3 copy-start.10
  130.4 1.3 copy-start.11
  133.1 3.3 %copy-start.2 = (bf16[1,1024,512]{1,2,0:T(8,128)(2,1)S(1)}, bf16[1,1024,512]{1,2,0:T(8,128)(2,1)}, u32[]{:S(2)}) copy-start(bf16[1,1024,512]{1,2,0:T(8,128)(2,1)} %copy.227) | copy-start | bytes 3145732
  133.1 3.3 %copy-start.49 = (f32[4]{0:T(128)S(1)}, f32[4]{0:T(128)}, u32[]{:S(2)}) copy-start(f32[4]{0:T(128)} %get-tuple-element.25) | copy-start | bytes 52
  133.1 3.3 %copy-start.50 = (f32[4]{0:T(128)S(1)}, f32[4]{0:T(128)}, u32[]{:S(2)}) copy-start(f32[4]{0:T(128)} %get-tuple-element.26) | copy-start | bytes 52
  133.1 3.3 %copy-start.51 = (f32[4]{0:T(128)S(1)}, f32[4]{0:T(128)}, u32[]{:S(2)}) copy-start(f32[4]{0:T(128)} %get-tuple-element.27) | copy-start | bytes 52
  133.1 3.3 %copy-start.52 = (f32[4]{0:T(128)S(1)}, f32[4]{0:T(128)}, u32[]{:S(2)}) copy-start(f32[4]{0:T(128)} %get-tuple-element.28) | copy-start | bytes 52
  134.1 2.3 %copy-start.3 = (f32[128,1024]{1,0:T(8,128)S(1)}, f32[128,1024]{1,0:T(8,128)}, u32[]{:S(2)}) copy-start(f32[128,1024]{1,0:T(8,128)} %copy.271) | copy-start | bytes 1572868
  135.2 1.3 copy-start.4
  136.4 1.9 %copy-start.43 = (f32[512]{0:T(512)S(1)}, f32[512]{0:T(512)}, u32[]{:S(2)}) copy-start(f32[512]{0:T(512)} %param.11) | copy-start | bytes 6148
Sparse Core Ops, SparseCore 0:
  32.0 26.9 all-gather.1
where the time goes:
time: 158 us; the launch traced here: 157 us
  local copies, waits for them, and re-layouts  52.8 us (33%)
  matrix products  38.1 us (24%)
  blocking collectives  28.5 us (18%)
  between operations  14.5 us (9%)
  waiting for transfers between devices  12.6 us (8%)
  other arithmetic  9 us (6%)
    all_to_all x1, blocking collectives, shards(): lax.all_to_all(stacked, 'uly', split_axis=2, concat_axis=1, tiled=True)  17.8 us
    unnamed x121, local copies, waits for them, and re-layouts  14.7 us
    another operation x9, local copies, waits for them, and re-layouts, shards(): jnp.stack([key_pad[start:start + KEY_BLOCK + col_lead] for start in range...  14.4 us
    all_gather x1, waiting for transfers between devices, shards(): lax.all_gather(jnp.stack([key_local, value_local]), 'ctx', axis=1, tiled=...  12.5 us
    dot_general x1, matrix products, group_logits(): jnp.einsum('ihad,nhard->hinr', shifted, keys_low, preferred_element_type=...  10.9 us
    all_to_all x1, blocking collectives, shards(): lax.all_to_all(attended, 'uly', split_axis=0, concat_axis=1, tiled=True)  10.7 us
    dot_general x1, matrix products, group_logits(): jnp.einsum('ihad,nhard->hinr', shifted, keys_high, preferred_element_type...  10.4 us
    dot_general x1, matrix products, convolved_keys(): jnp.einsum('harc,nchd->nhard', high, key_heads, preferred_element_type=jn...  8.7 us
  transfers between devices with their start and end apart: 2, of which 2 were waited for; matrix products, arithmetic and copies ran while one was open for 8% of the time, Pallas kernels for 0%

commit v1 on v0

--- a/solution.py
+++ b/solution.py
@@ -136,9 +136,23 @@
     query_first = ctx_place * shard_rows
     earlier = passed_along(query_local[shard_rows - row_lead :], "ctx", 1)
     query_ext = jnp.concatenate([earlier, query_local], axis=0)
-    key_all, value_all = lax.all_gather(
-        jnp.stack([key_local, value_local]), "ctx", axis=1, tiled=True
-    )
+
+    def step_on_sides_by_axis(inner_x, dim_i):
+        named_axis = "ctx"
+        dev_count = lax.axis_size(named_axis)
+        ledger = [(it, (it + 1) % dev_count) for it in range(dev_count)]
+        runs = [(it, (it - 1) % dev_count) for it in range(dev_count)]
+        ready, v_next = ([inner_x], [inner_x])
+        for _ in range(dev_count // 2):
+            ready.append(lax.ppermute(ready[-1], axis_name=named_axis, perm=ledger))
+        for _ in range((dev_count - 1) // 2):
+            v_next.append(lax.ppermute(v_next[-1], axis_name=named_axis, perm=runs))
+        plain = jnp.concatenate([*ready[::-1], *v_next[1:]], axis=dim_i)
+        return jnp.roll(
+            plain, (lax.axis_index(named_axis) - dev_count // 2) * inner_x.shape[dim_i], axis=dim_i
+        )
+
+    key_all, value_all = step_on_sides_by_axis(jnp.stack([key_local, value_local]), 1)
     seq_len = key_all.shape[0]
     key_pad = jnp.concatenate([jnp.zeros((col_lead, width), key_all.dtype), key_all], axis=0)
     key_windows = jnp.stack(

time: 158 us -> 154 us (0.975)
  blocking collectives: 28.5 us -> 8.81 us
  starting transfers between devices: 1.29 us -> 16 us
  between operations: 14.5 us -> 1.34 us
  local copies, waits for them, and re-layouts: 52.8 us -> 60.3 us
  waiting for transfers between devices: 12.6 us -> 18.1 us
    all_to_all x1 -> x0, blocking collectives: 17.8 us -> none  [shards(): lax.all_to_all(stacked, 'uly', split_axis=2, concat_axis=1, tiled=True)]
    all_gather x1 -> x0, waiting for transfers between devices: 12.5 us -> none  [shards(): lax.all_gather(jnp.stack([key_local, value_local]), 'ctx', axis=1, tiled=...]
    ppermute x0 -> x7, waiting for transfers between devices: none -> 10.2 us  [the longest x4 6.45 us: step_on_sides_by_axis(): ready.append(lax.ppermute(ready[-1], axis_name=named_axis, perm=ledger))]
    ppermute x0 -> x7, starting transfers between devices: none -> 8.4 us  [the longest x3 7.97 us: step_on_sides_by_axis(): v_next.append(lax.ppermute(v_next[-1], axis_name=named_axis, perm=runs))]
    all_to_all x0 -> x1, waiting for transfers between devices: none -> 7.91 us  [shards(): lax.all_to_all(stacked, 'uly', split_axis=2, concat_axis=1, tiled=True)]
    all_to_all x0 -> x1, starting transfers between devices: none -> 6.32 us  [shards(): lax.all_to_all(stacked, 'uly', split_axis=2, concat_axis=1, tiled=True)]
    unnamed x121 -> x162, local copies, waits for them, and re-layouts: 14.7 us -> 18.5 us
    another operation x7, local copies, waits for them, and re-layouts: 0.75 us -> 3.14 us  [shards(): jnp.stack([query_heads[row_lead - lag:row_lead - lag + shard_rows] for la...]
  transfers between devices with their start and end apart: 2 -> 9, of which waited for: 2 -> 4; matrix products, arithmetic and copies ran while one was open for 8% -> 13% of each run, Pallas kernels for 0% -> 0%
where the time goes in v1:
time: 154 us; the launch traced here: 153 us
  local copies, waits for them, and re-layouts  60.3 us (39%)
  matrix products  38.1 us (25%)
  waiting for transfers between devices  18.1 us (12%)
  starting transfers between devices  16 us (10%)
  other arithmetic  10.3 us (7%)
  blocking collectives  8.81 us (6%)
    unnamed x162, local copies, waits for them, and re-layouts  18.5 us
    another operation x9, local copies, waits for them, and re-layouts, shards(): jnp.stack([key_pad[start:start + KEY_BLOCK + col_lead] for start in range...  14.4 us
    dot_general x1, matrix products, group_logits(): jnp.einsum('ihad,nhard->hinr', shifted, keys_low, preferred_element_type=...  10.9 us
    dot_general x1, matrix products, group_logits(): jnp.einsum('ihad,nhard->hinr', shifted, keys_high, preferred_element_type...  10.4 us
    all_to_all x1, blocking collectives, shards(): lax.all_to_all(attended, 'uly', split_axis=0, concat_axis=1, tiled=True)  8.81 us
    dot_general x1, matrix products, convolved_keys(): jnp.einsum('harc,nchd->nhard', high, key_heads, preferred_element_type=jn...  8.66 us
    ppermute x3, starting transfers between devices, step_on_sides_by_axis(): v_next.append(lax.ppermute(v_next[-1], axis_name=named_axis, perm=runs))  7.97 us
    all_to_all x1, waiting for transfers between devices, shards(): lax.all_to_all(stacked, 'uly', split_axis=2, concat_axis=1, tiled=True)  7.91 us
  transfers between devices with their start and end apart: 9, of which 4 were waited for; matrix products, arithmetic and copies ran while one was open for 13% of the time, Pallas kernels for 0%

profile of v1, /device:TPU:0, one launch (start us, length us, event | category | flops | bytes accessed | tf_op | source)
XLA Modules:
  0.0 152.9 jit_solution(9388925561380246868)
XLA Ops:
  0.0 1.1 pad_maximum_fusion
  1.1 1.4 copy.223
  2.5 2.5 %reshape.295 = bf16[4,2,24576]{2,1,0:T(2,128)(2,1)} reshape(bf16[2048,3,32]{2,1,0:T(4,128)(2,1)S(1)} %bitcast.118) | data formatting | bytes 786432
  4.9 6.3 %all-to-all-start = ((bf16[4,2,24576]{2,1,0:T(2,128)(2,1)}), bf16[4,2,24576]{2,1,0:T(2,128)(2,1)S(1)}, u32[]{:S(2)}, u32[]{:S(2)}) async-start(bf16[4,2,24576]{2,1,0:T(2,128)(2,1)} %reshape.295), calls=%async_computation | async-start | bytes 786432 | tf_op jit(solution)/shard_map/all_to_all | solution.py:126
  11.3 0.8 fusion.129
  12.0 1.0 slice_reduce_fusion.17
  13.0 0.8 fusion.108
  13.8 1.3 fusion.84
  15.0 7.9 %all-to-all-done = bf16[4,2,24576]{2,1,0:T(2,128)(2,1)S(1)} async-done(((bf16[4,2,24576]{2,1,0:T(2,128)(2,1)}), bf16[4,2,24576]{2,1,0:T(2,128)(2,1)S(1)}, u32[]{:S(2)}, u32[]{:S(2)}) %all-to-all-start) | async-done | bytes 393248 | tf_op jit(solution)/shard_map/all_to_all | solution.py:126
  22.9 1.3 reshape.296
  24.3 1.2 copy.282
  25.8 0.7 pad_maximum_fusion.1
  26.5 1.8 %subtract_compare_fusion.5 = (pred[128,8,128]{0,2,1:T(8,128)(4,1)S(1)}, pred[128,8,128]{0,2,1:T(8,128)(4,1)S(1)}, pred[128,8,128]{0,2,1:T(8,128)(4,1)S(1)}, pred...) fusion(s32[8,128]{1,0:T(8,128)S(1)} %multiply_add_fusion, ...), kind=kLoop, calls=%fused_computation.29 | loop fusion | flops 917504 | bytes 791040 | tf_op jit(solution)/shard_map/ge | solution.py:104
  28.4 5.1 %collective-permute-done = bf16[2,128,512]{2,1,0:T(8,128)(2,1)S(1)} collective-permute-done((bf16[2,128,512]{2,1,0:T(8,128)(2,1)}, bf16[2,128,512]{2,1,0:T(8,128)(2,1)S(1)}, u32[]{:S(2)}, u32[]{:S(2)}) %collective-permute-start) | collective-permute-done | bytes 262176 | tf_op jit(solution)/shard_map/ppermute | solution.py:147
  33.4 0.8 slice_reduce_fusion.18
  35.4 0.7 copy.254
  36.1 0.7 copy.253
  37.5 0.7 copy.251
  38.2 0.7 copy.250
  39.5 2.6 %collective-permute-start.4 = (bf16[2,128,512]{2,1,0:T(8,128)(2,1)}, bf16[2,128,512]{2,1,0:T(8,128)(2,1)S(1)}, u32[]{:S(2)}, u32[]{:S(2)}) collective-permute-start(bf16[2,128,512]{2,1,0:T(8,128)(2,1)} %pad_maximum_fusion.1), channel_id=1, source_target_pairs={{0,28},{4,0},{8,4},{12,8},{16,12},{20,16},{24,20},{28,24},{1,29},{... | collective-permute-start | bytes 786440 | tf_op jit(solution)/shard_map/ppermute | solution.py:149
  42.3 1.3 collective-permute-start.7
  44.7 0.8 pad_maximum_fusion.3
  46.2 0.8 copy.238
  47.0 2.6 %collective-permute-start.5 = (bf16[2,128,512]{2,1,0:T(8,128)(2,1)S(1)}, bf16[2,128,512]{2,1,0:T(8,128)(2,1)S(1)}, u32[]{:S(2)}, u32[]{:S(2)}) collective-permute-start(bf16[2,128,512]{2,1,0:T(8,128)(2,1)S(1)} %collective-permute-done.4), channel_id=1, source_target_pairs={{0,28},{4,0},{8,4},{12,8},{16,12},{20,16},{24,20},{28,24},{1,29},{... | collective-permute-start | bytes 786440 | tf_op jit(solution)/shard_map/ppermute | solution.py:149
  49.6 1.4 collective-permute-done.2
  51.0 0.9 constant_dynamic-update-slice_fusion.18
  51.9 0.8 copy.233
  52.7 1.0 copy.239
  53.7 0.8 copy.234
  54.5 1.0 copy.240
  55.5 1.3 concatenate.26
  56.9 2.7 %collective-permute-start.6 = (bf16[2,128,512]{2,1,0:T(8,128)(2,1)S(1)}, bf16[2,128,512]{2,1,0:T(8,128)(2,1)S(1)}, u32[]{:S(2)}, u32[]{:S(2)}) collective-permute-start(bf16[2,128,512]{2,1,0:T(8,128)(2,1)S(1)} %collective-permute-done.5), channel_id=1, source_target_pairs={{0,28},{4,0},{8,4},{12,8},{16,12},{20,16},{24,20},{28,24},{1,29},{... | collective-permute-start | bytes 786440 | tf_op jit(solution)/shard_map/ppermute | solution.py:149
  59.7 3.7 %collective-permute-done.6 = bf16[2,128,512]{2,1,0:T(8,128)(2,1)S(1)} collective-permute-done((bf16[2,128,512]{2,1,0:T(8,128)(2,1)S(1)}, bf16[2,128,512]{2,1,0:T(8,128)(2,1)S(1)}, u32[]{:S(2)}, u32[]{:S(2)}) %collective-permute-start.6) | collective-permute-done | bytes 262176 | tf_op jit(solution)/shard_map/ppermute | solution.py:149
  63.9 1.8 %copy-done = bf16[2,2048,512]{2,1,0:T(8,128)(2,1)} copy-done((bf16[2,2048,512]{2,1,0:T(8,128)(2,1)}, bf16[2,2048,512]{2,1,0:T(8,128)(2,1)S(1)}, u32[]{:S(2)}) %copy-start) | copy-done | bytes 4194328
  66.3 1.6 %stack.75 = bf16[1,138,4,128]{3,2,1,0:T(4,128)(2,1)} reshape(bf16[138,512]{1,0:T(8,128)(2,1)} %pad_slice_fusion) | data formatting | bytes 282624 | tf_op jit(solution)/shard_map/stack | solution.py:158
  67.9 1.6 %copy_dynamic-update-slice_fusion.7 = bf16[8,138,4,128]{3,1,0,2:T(8,128)(2,1)} fusion(bf16[1,138,4,128]{3,2,1,0:T(4,128)(2,1)} %stack.75), kind=kLoop, calls=%fused_computation.138 | loop fusion | bytes 288768
  69.5 2.4 %constant_dynamic-slice_fusion.7 = (bf16[1,138,512]{2,1,0:T(8,128)(2,1)}, bf16[1,138,512]{2,1,0:T(8,128)(2,1)}, bf16[1,138,512]{2,1,0:T(8,128)(2,1)}, bf16[1,138...) fusion(bf16[2,2048,512]{2,1,0:T(8,128)(2,1)} %copy-done, ...), kind=kLoop, calls=%fused_computation.188 | loop fusion | bytes 1978396 | tf_op jit(solution)/shard_map/slice | solution.py:159
  72.0 1.6 %stack.76 = bf16[1,138,4,128]{3,2,1,0:T(4,128)(2,1)} reshape(bf16[1,138,512]{2,1,0:T(8,128)(2,1)} %get-tuple-element.35) | data formatting | bytes 282624 | tf_op jit(solution)/shard_map/stack | solution.py:158
  73.6 1.6 %stack.77 = bf16[1,138,4,128]{3,2,1,0:T(4,128)(2,1)} reshape(bf16[1,138,512]{2,1,0:T(8,128)(2,1)} %get-tuple-element.34) | data formatting | bytes 282624 | tf_op jit(solution)/shard_map/stack | solution.py:158
  75.2 1.6 %stack.78 = bf16[1,138,4,128]{3,2,1,0:T(4,128)(2,1)} reshape(bf16[1,138,512]{2,1,0:T(8,128)(2,1)} %get-tuple-element.33) | data formatting | bytes 282624 | tf_op jit(solution)/shard_map/stack | solution.py:158
  76.8 1.6 %stack.79 = bf16[1,138,4,128]{3,2,1,0:T(4,128)(2,1)} reshape(bf16[1,138,512]{2,1,0:T(8,128)(2,1)} %get-tuple-element.32) | data formatting | bytes 282624 | tf_op jit(solution)/shard_map/stack | solution.py:158
  78.4 1.6 %stack.80 = bf16[1,138,4,128]{3,2,1,0:T(4,128)(2,1)} reshape(bf16[1,138,512]{2,1,0:T(8,128)(2,1)} %get-tuple-element.31) | data formatting | bytes 282624 | tf_op jit(solution)/shard_map/stack | solution.py:158
  80.0 1.6 %stack.81 = bf16[1,138,4,128]{3,2,1,0:T(4,128)(2,1)} reshape(bf16[1,138,512]{2,1,0:T(8,128)(2,1)} %get-tuple-element.30) | data formatting | bytes 282624 | tf_op jit(solution)/shard_map/stack | solution.py:158
  81.6 1.6 %stack.82 = bf16[1,138,4,128]{3,2,1,0:T(4,128)(2,1)} reshape(bf16[1,138,512]{2,1,0:T(8,128)(2,1)} %get-tuple-element.29) | data formatting | bytes 282624 | tf_op jit(solution)/shard_map/stack | solution.py:158
  83.2 1.6 %copy_dynamic-update-slice_fusion.6 = bf16[8,138,4,128]{3,1,0,2:T(8,128)(2,1)} fusion(bf16[8,138,4,128]{3,1,0,2:T(8,128)(2,1)} %copy_dynamic-update-slice_fusion.7, bf16[1,138,4,128]{3,2,1,0:T(4,128)(2,1)} %stack.76), kind=kLoop, calls=%fused_computation.137 | loop fusion | bytes 288768
  84.8 1.6 %copy_dynamic-update-slice_fusion.5 = bf16[8,138,4,128]{3,1,0,2:T(8,128)(2,1)} fusion(bf16[8,138,4,128]{3,1,0,2:T(8,128)(2,1)} %copy_dynamic-update-slice_fusion.6, bf16[1,138,4,128]{3,2,1,0:T(4,128)(2,1)} %stack.77), kind=kLoop, calls=%fused_computation.136 | loop fusion | bytes 288768
  86.3 1.6 %copy_dynamic-update-slice_fusion.4 = bf16[8,138,4,128]{3,1,0,2:T(8,128)(2,1)} fusion(bf16[8,138,4,128]{3,1,0,2:T(8,128)(2,1)} %copy_dynamic-update-slice_fusion.5, bf16[1,138,4,128]{3,2,1,0:T(4,128)(2,1)} %stack.78), kind=kLoop, calls=%fused_computation.135 | loop fusion | bytes 288768
  87.9 1.6 %copy_dynamic-update-slice_fusion.3 = bf16[8,138,4,128]{3,1,0,2:T(8,128)(2,1)} fusion(bf16[8,138,4,128]{3,1,0,2:T(8,128)(2,1)} %copy_dynamic-update-slice_fusion.4, bf16[1,138,4,128]{3,2,1,0:T(4,128)(2,1)} %stack.79), kind=kLoop, calls=%fused_computation.134 | loop fusion | bytes 288768
  89.5 1.6 %copy_dynamic-update-slice_fusion.2 = bf16[8,138,4,128]{3,1,0,2:T(8,128)(2,1)} fusion(bf16[8,138,4,128]{3,1,0,2:T(8,128)(2,1)} %copy_dynamic-update-slice_fusion.3, bf16[1,138,4,128]{3,2,1,0:T(4,128)(2,1)} %stack.80), kind=kLoop, calls=%fused_computation.133 | loop fusion | bytes 288768
  91.1 1.6 %copy_dynamic-update-slice_fusion.1 = bf16[8,138,4,128]{3,1,0,2:T(8,128)(2,1)} fusion(bf16[8,138,4,128]{3,1,0,2:T(8,128)(2,1)} %copy_dynamic-update-slice_fusion.2, bf16[1,138,4,128]{3,2,1,0:T(4,128)(2,1)} %stack.81), kind=kLoop, calls=%fused_computation.132 | loop fusion | bytes 288768
  92.7 1.6 %copy_dynamic-update-slice_fusion = bf16[8,138,4,128]{3,1,0,2:T(8,128)(2,1)} fusion(bf16[8,138,4,128]{3,1,0,2:T(8,128)(2,1)} %copy_dynamic-update-slice_fusion.1, bf16[1,138,4,128]{3,2,1,0:T(4,128)(2,1)} %stack.82), kind=kLoop, calls=%fused_computation.131 | loop fusion | bytes 288768 | tf_op jit(solution)/shard_map/stack | solution.py:158
  94.4 8.7 %fusion.17 = f32[4,8,128,6,128]{4,2,3,1,0:T(8,128)} fusion(bf16[8,138,4,128]{3,1,0,2:T(8,128)(2,1)} %copy_dynamic-update-slice_fusion, f32[4,6]{1,0:T(4,128)S(1)} %bitcast.139, f32[4,6]{1,0:T(4,128)S(1)} %bitcast.141, f32[4,6]{1,0:T(4,128)S(1)} %bitcast.143, f32[4,6]{1,0:T(4,128)S(1)} %bitcast.145, f32[4,6]{1,0:T(4,128)} %bitcast.147, ...), kind=kOutput, calls=%fused_computation.32 | convolution fusion | flops 873732096 | bytes 13908768 | tf_op jit(solution)/shard_map/harc,nchd->nhard/dot_general | solution.py:46
  103.3 6.3 %fusion.15 = f32[4,8,128,6,128]{4,2,3,1,0:T(8,128)} fusion(bf16[8,138,4,128]{3,1,0,2:T(8,128)(2,1)S(1)} %copy-done.1, f32[4,6]{1,0:T(4,128)S(1)} %bitcast.140, f32[4,6]{1,0:T(4,128)S(1)} %bitcast.142, f32[4,6]{1,0:T(4,128)S(1)} %bitcast.144, f32[4,6]{1,0:T(4,128)S(1)} %bitcast.146, f32[4,6]{1,0:T(4,128)S(1)} %bitcast.148, f32[4,6]{1,0:T(4,128)S(1)} %bitcast.150, ...), kind=kOutput, calls=%fused_computation.30 | convolution fusion | flops 874156032 | bytes 13908768 | tf_op jit(solution)/shard_map/harc,nchd->nhard/dot_general | solution.py:48
  109.6 1.4 copy.227
  111.9 0.8 fusion.90
  113.3 10.9 %fusion.1 = f32[4,128,8,128,1]{1,3,4,2,0:T(8,128)S(1)} fusion(f32[4,8,128,6,128]{4,2,3,1,0:T(8,128)} %fusion.17, f32[4,8,128,6,128]{4,2,3,1,0:T(8,128)} %fusion.15, bf16[128,4,6,128]{3,0,2,1:T(8,128)(2,1)S(1)} %constant_dynamic-update-slice_fusion.16), kind=kOutput, calls=%fused_computation.3 | convolution fusion | flops 817889280 | bytes 28049408 | tf_op jit(solution)/shard_map/ihad,nhard->hinr/dot_general | solution.py:84
  124.6 10.4 %fusion.85 = (f32[4,128]{1,0:T(4,128)S(1)}, f32[4,128,8,128]{1,3,2,0:T(8,128)S(1)}) fusion(f32[4,128]{1,0:T(4,128)S(1)} %get-tuple-element.74, pred[128,8,128]{0,2,1:T(8,128)(4,1)S(1)} %get-tuple-element.69, f32[4,128]{1,0:T(4,128)S(1)} %get-tuple-element.67, pred[128,8,128]{0,2,1:T(8,128)(4,1)S(1)} %get-tuple-element.70, ...), kind=kOutput, calls=%fused_computation.115 | convolution fusion | flops 821558784 | bytes 30945280 | tf_op jit(solution)/shard_map/ihad,nhard->hinr/dot_general | solution.py:82
  135.1 1.3 exponential_reduce_fusion
  136.4 1.3 fusion.13
  137.9 1.0 copy.271
  138.9 1.0 copy.270
  139.9 1.0 copy.269
  141.2 1.8 %multiply_reduce_fusion = (f32[128,4]{0,1:T(4,128)S(1)}, f32[128,4,128]{0,2,1:T(8,128)S(1)}) fusion(bf16[1024,4,128]{0,2,1:T(8,128)(2,1)S(1)} %bitcast.129, f32[128,1024]{1,0:T(8,128)S(1)} %copy-done.5, f32[4]{0:T(128)S(1)} %copy-done.64, f32[128,1024]{1,0:T(8,128)S(1)} %copy-done.6, f32[4]{0:T(128)S(1)} %copy-done.65, f32[128,1024]{1,0:T(8,128)} %copy.269, ...), kind=kOutput, calls=%fused_computation.127 | convolution fusion | flops 138542592 | bytes 3409984 | tf_op jit(solution)/shard_map/hik,khd->ihd/dot_general | solution.py:114
  143.4 8.8 %all_to_all.34 = bf16[4,32,512]{2,1,0:T(8,128)(2,1)S(1)} all-to-all(bf16[4,32,512]{2,1,0:T(8,128)(2,1)S(1)} %all_to_all.28), channel_id=1, replica_groups=mesh['ctx'=8,'uly'=4] {'uly'}, dimensions={0} | all-to-all | bytes 262144 | tf_op jit(solution)/shard_map/all_to_all | solution.py:194
  (214 shorter events, 9.0 us)
Async XLA Ops:
  2.4 8.8 %copy-start.25 = (f32[4,6,11]{2,0,1:T(4,128)S(1)}, f32[4,6,11]{2,0,1:T(4,128)}, u32[]{:S(2)}) copy-start(f32[4,6,11]{2,0,1:T(4,128)} %param.9) | copy-start | bytes 3172
  4.9 18.0 %all-to-all-start = ((bf16[4,2,24576]{2,1,0:T(2,128)(2,1)}), bf16[4,2,24576]{2,1,0:T(2,128)(2,1)S(1)}, u32[]{:S(2)}, u32[]{:S(2)}) async-start(bf16[4,2,24576]{2,1,0:T(2,128)(2,1)} %reshape.295), calls=%async_computation | async-start | bytes 786432 | tf_op jit(solution)/shard_map/all_to_all | solution.py:126
  12.0 13.5 %copy-start.62 = (s32[128]{0:T(128)}, s32[128]{0:T(128)S(1)}, u32[]{:S(2)}) copy-start(s32[128]{0:T(128)S(1)} %iota_add_fusion.1) | copy-start | bytes 1540
  24.3 9.2 %copy-start.44 = (f32[4,4]{1,0:T(4,128)S(1)}, f32[4,4]{1,0:T(4,128)}, u32[]{:S(2)}) copy-start(f32[4,4]{1,0:T(4,128)} %param.10) | copy-start | bytes 196
  25.5 8.9 %copy-start.42 = (f32[4,6,1]{2,0,1:T(4,128)S(1)}, f32[4,6,1]{2,0,1:T(4,128)}, u32[]{:S(2)}) copy-start(f32[4,6,1]{2,0,1:T(4,128)} %get-tuple-element.57) | copy-start | bytes 292
  25.5 9.0 %copy-start.41 = (f32[4,6,1]{2,0,1:T(4,128)S(1)}, f32[4,6,1]{2,0,1:T(4,128)}, u32[]{:S(2)}) copy-start(f32[4,6,1]{2,0,1:T(4,128)} %get-tuple-element.58) | copy-start | bytes 292
  25.5 9.1 %copy-start.40 = (f32[4,6,1]{2,0,1:T(4,128)S(1)}, f32[4,6,1]{2,0,1:T(4,128)}, u32[]{:S(2)}) copy-start(f32[4,6,1]{2,0,1:T(4,128)} %get-tuple-element.59) | copy-start | bytes 292
  25.5 9.2 %copy-start.39 = (f32[4,6,1]{2,0,1:T(4,128)S(1)}, f32[4,6,1]{2,0,1:T(4,128)}, u32[]{:S(2)}) copy-start(f32[4,6,1]{2,0,1:T(4,128)} %get-tuple-element.60) | copy-start | bytes 292
  25.5 9.9 %copy-start.38 = (f32[4,6,1]{2,0,1:T(4,128)S(1)}, f32[4,6,1]{2,0,1:T(4,128)}, u32[]{:S(2)}) copy-start(f32[4,6,1]{2,0,1:T(4,128)} %get-tuple-element.61) | copy-start | bytes 292
  25.5 10.6 %copy-start.37 = (f32[4,6,1]{2,0,1:T(4,128)S(1)}, f32[4,6,1]{2,0,1:T(4,128)}, u32[]{:S(2)}) copy-start(f32[4,6,1]{2,0,1:T(4,128)} %get-tuple-element.62) | copy-start | bytes 292
  25.5 11.2 %copy-start.36 = (f32[4,6,1]{2,0,1:T(4,128)S(1)}, f32[4,6,1]{2,0,1:T(4,128)}, u32[]{:S(2)}) copy-start(f32[4,6,1]{2,0,1:T(4,128)} %get-tuple-element.63) | copy-start | bytes 292
  25.6 11.9 %copy-start.35 = (f32[4,6,1]{2,0,1:T(4,128)S(1)}, f32[4,6,1]{2,0,1:T(4,128)}, u32[]{:S(2)}) copy-start(f32[4,6,1]{2,0,1:T(4,128)} %get-tuple-element.64) | copy-start | bytes 292
  25.6 12.6 %copy-start.34 = (f32[4,6,1]{2,0,1:T(4,128)S(1)}, f32[4,6,1]{2,0,1:T(4,128)}, u32[]{:S(2)}) copy-start(f32[4,6,1]{2,0,1:T(4,128)} %get-tuple-element.65) | copy-start | bytes 292
  25.6 13.3 %copy-start.33 = (f32[4,6,1]{2,0,1:T(4,128)S(1)}, f32[4,6,1]{2,0,1:T(4,128)}, u32[]{:S(2)}) copy-start(f32[4,6,1]{2,0,1:T(4,128)} %get-tuple-element.55) | copy-start | bytes 292
  26.5 6.9 %collective-permute-start = (bf16[2,128,512]{2,1,0:T(8,128)(2,1)}, bf16[2,128,512]{2,1,0:T(8,128)(2,1)S(1)}, u32[]{:S(2)}, u32[]{:S(2)}) collective-permute-start(bf16[2,128,512]{2,1,0:T(8,128)(2,1)} %pad_maximum_fusion.1), channel_id=1, source_target_pairs={{0,4},{4,8},{8,12},{12,16},{16,20},{20,24},{24,28},{28,0},{1,5},{5... | collective-permute-start | bytes 786440 | tf_op jit(solution)/shard_map/ppermute | solution.py:147
  33.4 10.8 %collective-permute-start.1 = (bf16[2,128,512]{2,1,0:T(8,128)(2,1)S(1)}, bf16[2,128,512]{2,1,0:T(8,128)(2,1)S(1)}, u32[]{:S(2)}, u32[]{:S(2)}) collective-permute-start(bf16[2,128,512]{2,1,0:T(8,128)(2,1)S(1)} %collective-permute-done), channel_id=1, source_target_pairs={{0,4},{4,8},{8,12},{12,16},{16,20},{20,24},{24,28},{28,0},{1,5},{5... | collective-permute-start | bytes 786440 | tf_op jit(solution)/shard_map/ppermute | solution.py:147
  39.5 7.4 %collective-permute-start.4 = (bf16[2,128,512]{2,1,0:T(8,128)(2,1)}, bf16[2,128,512]{2,1,0:T(8,128)(2,1)S(1)}, u32[]{:S(2)}, u32[]{:S(2)}) collective-permute-start(bf16[2,128,512]{2,1,0:T(8,128)(2,1)} %pad_maximum_fusion.1), channel_id=1, source_target_pairs={{0,28},{4,0},{8,4},{12,8},{16,12},{20,16},{24,20},{28,24},{1,29},{... | collective-permute-start | bytes 786440 | tf_op jit(solution)/shard_map/ppermute | solution.py:149
  42.3 2.5 %collective-permute-start.7 = (bf16[5,512]{1,0:T(8,128)(2,1)S(1)}, bf16[5,512]{1,0:T(8,128)(2,1)S(1)}, u32[]{:S(2)}, u32[]{:S(2)}) collective-permute-start(bf16[5,512]{1,0:T(8,128)(2,1)S(1)} %slice.356), channel_id=1, source_target_pairs={{0,4},{4,8},{8,12},{12,16},{16,20},{20,24},{24,28},{1,5},{5,9},{9,... | collective-permute-start | bytes 15368 | tf_op jit(solution)/shard_map/ppermute | solution.py:19
  44.3 6.7 %collective-permute-start.2 = (bf16[2,128,512]{2,1,0:T(8,128)(2,1)S(1)}, bf16[2,128,512]{2,1,0:T(8,128)(2,1)S(1)}, u32[]{:S(2)}, u32[]{:S(2)}) collective-permute-start(bf16[2,128,512]{2,1,0:T(8,128)(2,1)S(1)} %collective-permute-done.1), channel_id=1, source_target_pairs={{0,4},{4,8},{8,12},{12,16},{16,20},{20,24},{24,28},{28,0},{1,5},{5... | collective-permute-start | bytes 786440 | tf_op jit(solution)/shard_map/ppermute | solution.py:147
  45.5 6.4 %copy-start.4 = (bf16[128,512]{1,0:T(8,128)(2,1)S(1)}, bf16[128,512]{1,0:T(8,128)(2,1)}, u32[]{:S(2)}) copy-start(bf16[128,512]{1,0:T(8,128)(2,1)} %get-tuple-element.54) | copy-start | bytes 393220
  47.0 9.9 %collective-permute-start.5 = (bf16[2,128,512]{2,1,0:T(8,128)(2,1)S(1)}, bf16[2,128,512]{2,1,0:T(8,128)(2,1)S(1)}, u32[]{:S(2)}, u32[]{:S(2)}) collective-permute-start(bf16[2,128,512]{2,1,0:T(8,128)(2,1)S(1)} %collective-permute-done.4), channel_id=1, source_target_pairs={{0,28},{4,0},{8,4},{12,8},{16,12},{20,16},{24,20},{28,24},{1,29},{... | collective-permute-start | bytes 786440 | tf_op jit(solution)/shard_map/ppermute | solution.py:149
  51.0 8.6 %collective-permute-start.3 = (bf16[2,128,512]{2,1,0:T(8,128)(2,1)S(1)}, bf16[2,128,512]{2,1,0:T(8,128)(2,1)S(1)}, u32[]{:S(2)}, u32[]{:S(2)}) collective-permute-start(bf16[2,128,512]{2,1,0:T(8,128)(2,1)S(1)} %collective-permute-done.2), channel_id=1, source_target_pairs={{0,4},{4,8},{8,12},{12,16},{16,20},{20,24},{24,28},{28,0},{1,5},{5... | collective-permute-start | bytes 786440 | tf_op jit(solution)/shard_map/ppermute | solution.py:147
  56.9 6.6 %collective-permute-start.6 = (bf16[2,128,512]{2,1,0:T(8,128)(2,1)S(1)}, bf16[2,128,512]{2,1,0:T(8,128)(2,1)S(1)}, u32[]{:S(2)}, u32[]{:S(2)}) collective-permute-start(bf16[2,128,512]{2,1,0:T(8,128)(2,1)S(1)} %collective-permute-done.5), channel_id=1, source_target_pairs={{0,28},{4,0},{8,4},{12,8},{16,12},{20,16},{24,20},{28,24},{1,29},{... | collective-permute-start | bytes 786440 | tf_op jit(solution)/shard_map/ppermute | solution.py:149
  94.3 8.8 %copy-start.1 = (bf16[8,138,4,128]{3,1,0,2:T(8,128)(2,1)S(1)}, bf16[8,138,4,128]{3,1,0,2:T(8,128)(2,1)}, u32[]{:S(2)}) copy-start(bf16[8,138,4,128]{3,1,0,2:T(8,128)(2,1)} %copy_dynamic-update-slice_fusion) | copy-start | bytes 3391492
  94.3 8.8 %copy-start.14 = (pred[128,138]{0,1:T(8,128)(4,1)S(1)}, pred[128,138]{0,1:T(8,128)(4,1)}, u32[]{:S(2)}) copy-start(pred[128,138]{0,1:T(8,128)(4,1)} %get-tuple-element.81) | copy-start | bytes 52996
  94.3 8.8 %copy-start.15 = (pred[128,138]{0,1:T(8,128)(4,1)S(1)}, pred[128,138]{0,1:T(8,128)(4,1)}, u32[]{:S(2)}) copy-start(pred[128,138]{0,1:T(8,128)(4,1)} %get-tuple-element.82) | copy-start | bytes 52996
  94.3 8.8 %copy-start.16 = (pred[128,138]{0,1:T(8,128)(4,1)S(1)}, pred[128,138]{0,1:T(8,128)(4,1)}, u32[]{:S(2)}) copy-start(pred[128,138]{0,1:T(8,128)(4,1)} %get-tuple-element.83) | copy-start | bytes 52996
  94.3 8.8 %copy-start.17 = (pred[128,138]{0,1:T(8,128)(4,1)S(1)}, pred[128,138]{0,1:T(8,128)(4,1)}, u32[]{:S(2)}) copy-start(pred[128,138]{0,1:T(8,128)(4,1)} %get-tuple-element.84) | copy-start | bytes 52996
  94.3 8.8 %copy-start.18 = (pred[128,138]{0,1:T(8,128)(4,1)S(1)}, pred[128,138]{0,1:T(8,128)(4,1)}, u32[]{:S(2)}) copy-start(pred[128,138]{0,1:T(8,128)(4,1)} %get-tuple-element.85) | copy-start | bytes 52996
  94.3 8.8 %copy-start.19 = (pred[128,138]{0,1:T(8,128)(4,1)S(1)}, pred[128,138]{0,1:T(8,128)(4,1)}, u32[]{:S(2)}) copy-start(pred[128,138]{0,1:T(8,128)(4,1)} %get-tuple-element.86) | copy-start | bytes 52996
  94.3 8.8 %copy-start.20 = (pred[128,138]{0,1:T(8,128)(4,1)S(1)}, pred[128,138]{0,1:T(8,128)(4,1)}, u32[]{:S(2)}) copy-start(pred[128,138]{0,1:T(8,128)(4,1)} %get-tuple-element.87) | copy-start | bytes 52996
  94.3 8.8 %copy-start.21 = (pred[128,138]{0,1:T(8,128)(4,1)S(1)}, pred[128,138]{0,1:T(8,128)(4,1)}, u32[]{:S(2)}) copy-start(pred[128,138]{0,1:T(8,128)(4,1)} %get-tuple-element.88) | copy-start | bytes 52996
  94.3 8.8 %copy-start.22 = (pred[128,138]{0,1:T(8,128)(4,1)S(1)}, pred[128,138]{0,1:T(8,128)(4,1)}, u32[]{:S(2)}) copy-start(pred[128,138]{0,1:T(8,128)(4,1)} %get-tuple-element.89) | copy-start | bytes 52996
  94.4 8.8 %copy-start.23 = (pred[128,138]{0,1:T(8,128)(4,1)S(1)}, pred[128,138]{0,1:T(8,128)(4,1)}, u32[]{:S(2)}) copy-start(pred[128,138]{0,1:T(8,128)(4,1)} %get-tuple-element.90) | copy-start | bytes 52996
  94.4 8.8 %copy-start.24 = (pred[128,138]{0,1:T(8,128)(4,1)S(1)}, pred[128,138]{0,1:T(8,128)(4,1)}, u32[]{:S(2)}) copy-start(pred[128,138]{0,1:T(8,128)(4,1)} %get-tuple-element.91) | copy-start | bytes 52996
  94.4 8.8 %copy-start.26 = (f32[4,6,1]{1,0,2:T(4,128)S(1)}, f32[4,6,1]{1,0,2:T(4,128)}, u32[]{:S(2)}) copy-start(f32[4,6,1]{1,0,2:T(4,128)} %copy.255) | copy-start | bytes 292
  94.4 8.8 %copy-start.27 = (f32[4,6,1]{1,0,2:T(4,128)S(1)}, f32[4,6,1]{1,0,2:T(4,128)}, u32[]{:S(2)}) copy-start(f32[4,6,1]{1,0,2:T(4,128)} %copy.254) | copy-start | bytes 292
  94.4 8.8 %copy-start.28 = (f32[4,6,1]{1,0,2:T(4,128)S(1)}, f32[4,6,1]{1,0,2:T(4,128)}, u32[]{:S(2)}) copy-start(f32[4,6,1]{1,0,2:T(4,128)} %copy.253) | copy-start | bytes 292
  94.4 8.8 %copy-start.29 = (f32[4,6,1]{1,0,2:T(4,128)S(1)}, f32[4,6,1]{1,0,2:T(4,128)}, u32[]{:S(2)}) copy-start(f32[4,6,1]{1,0,2:T(4,128)} %copy.252) | copy-start | bytes 292
  94.4 8.8 %copy-start.30 = (f32[4,6,1]{1,0,2:T(4,128)S(1)}, f32[4,6,1]{1,0,2:T(4,128)}, u32[]{:S(2)}) copy-start(f32[4,6,1]{1,0,2:T(4,128)} %copy.251) | copy-start | bytes 292
  94.4 8.8 %copy-start.31 = (f32[4,6,1]{1,0,2:T(4,128)S(1)}, f32[4,6,1]{1,0,2:T(4,128)}, u32[]{:S(2)}) copy-start(f32[4,6,1]{1,0,2:T(4,128)} %copy.250) | copy-start | bytes 292
  94.4 8.8 %copy-start.32 = (f32[4,6,1]{1,0,2:T(4,128)S(1)}, f32[4,6,1]{1,0,2:T(4,128)}, u32[]{:S(2)}) copy-start(f32[4,6,1]{1,0,2:T(4,128)} %copy.249) | copy-start | bytes 292
  113.2 11.0 %copy-start.46 = (f32[4]{0:T(128)S(1)}, f32[4]{0:T(128)}, u32[]{:S(2)}) copy-start(f32[4]{0:T(128)} %get-tuple-element.11) | copy-start | bytes 52
  113.2 11.0 %copy-start.47 = (f32[4]{0:T(128)S(1)}, f32[4]{0:T(128)}, u32[]{:S(2)}) copy-start(f32[4]{0:T(128)} %get-tuple-element.12) | copy-start | bytes 52
  113.2 11.0 %copy-start.48 = (f32[4]{0:T(128)S(1)}, f32[4]{0:T(128)}, u32[]{:S(2)}) copy-start(f32[4]{0:T(128)} %get-tuple-element.13) | copy-start | bytes 52
  113.2 11.0 %copy-start.49 = (f32[4]{0:T(128)S(1)}, f32[4]{0:T(128)}, u32[]{:S(2)}) copy-start(f32[4]{0:T(128)} %get-tuple-element.16) | copy-start | bytes 52
  113.2 11.0 %copy-start.50 = (f32[4]{0:T(128)S(1)}, f32[4]{0:T(128)}, u32[]{:S(2)}) copy-start(f32[4]{0:T(128)} %get-tuple-element.17) | copy-start | bytes 52
  113.2 11.0 %copy-start.51 = (f32[4]{0:T(128)S(1)}, f32[4]{0:T(128)}, u32[]{:S(2)}) copy-start(f32[4]{0:T(128)} %get-tuple-element.20) | copy-start | bytes 52
  113.2 11.1 %copy-start.52 = (f32[4]{0:T(128)S(1)}, f32[4]{0:T(128)}, u32[]{:S(2)}) copy-start(f32[4]{0:T(128)} %get-tuple-element.15) | copy-start | bytes 52
  113.2 11.1 %copy-start.53 = (f32[4]{0:T(128)S(1)}, f32[4]{0:T(128)}, u32[]{:S(2)}) copy-start(f32[4]{0:T(128)} %get-tuple-element.19) | copy-start | bytes 52
  113.2 11.1 %copy-start.54 = (f32[4]{0:T(128)S(1)}, f32[4]{0:T(128)}, u32[]{:S(2)}) copy-start(f32[4]{0:T(128)} %get-tuple-element.22) | copy-start | bytes 52
  113.3 11.1 %copy-start.55 = (f32[4]{0:T(128)S(1)}, f32[4]{0:T(128)}, u32[]{:S(2)}) copy-start(f32[4]{0:T(128)} %get-tuple-element.24) | copy-start | bytes 52
  113.3 11.2 %copy-start.57 = (f32[4]{0:T(128)S(1)}, f32[4]{0:T(128)}, u32[]{:S(2)}) copy-start(f32[4]{0:T(128)} %get-tuple-element.10) | copy-start | bytes 52
  113.3 11.2 %copy-start.58 = (f32[4]{0:T(128)S(1)}, f32[4]{0:T(128)}, u32[]{:S(2)}) copy-start(f32[4]{0:T(128)} %get-tuple-element.14) | copy-start | bytes 52
  113.3 11.2 %copy-start.59 = (f32[4]{0:T(128)S(1)}, f32[4]{0:T(128)}, u32[]{:S(2)}) copy-start(f32[4]{0:T(128)} %get-tuple-element.18) | copy-start | bytes 52
  113.3 11.2 %copy-start.60 = (f32[4]{0:T(128)S(1)}, f32[4]{0:T(128)}, u32[]{:S(2)}) copy-start(f32[4]{0:T(128)} %get-tuple-element.21) | copy-start | bytes 52
  113.3 11.2 %copy-start.61 = (f32[4]{0:T(128)S(1)}, f32[4]{0:T(128)}, u32[]{:S(2)}) copy-start(f32[4]{0:T(128)} %get-tuple-element.23) | copy-start | bytes 52
  113.3 11.3 %copy-start.2 = (pred[128,8,128]{0,2,1:T(8,128)(4,1)S(1)}, pred[128,8,128]{0,2,1:T(8,128)(4,1)}, u32[]{:S(2)}) copy-start(pred[128,8,128]{0,2,1:T(8,128)(4,1)} %get-tuple-element.73) | copy-start | bytes 393220
  137.8 3.3 %copy-start.3 = (bf16[1,1024,512]{1,2,0:T(8,128)(2,1)S(1)}, bf16[1,1024,512]{1,2,0:T(8,128)(2,1)}, u32[]{:S(2)}) copy-start(bf16[1,1024,512]{1,2,0:T(8,128)(2,1)} %copy.227) | copy-start | bytes 3145732
  137.8 3.3 %copy-start.63 = (f32[4]{0:T(128)S(1)}, f32[4]{0:T(128)}, u32[]{:S(2)}) copy-start(f32[4]{0:T(128)} %get-tuple-element.25) | copy-start | bytes 52
  137.9 3.3 %copy-start.64 = (f32[4]{0:T(128)S(1)}, f32[4]{0:T(128)}, u32[]{:S(2)}) copy-start(f32[4]{0:T(128)} %get-tuple-element.26) | copy-start | bytes 52
  137.9 3.3 %copy-start.65 = (f32[4]{0:T(128)S(1)}, f32[4]{0:T(128)}, u32[]{:S(2)}) copy-start(f32[4]{0:T(128)} %get-tuple-element.27) | copy-start | bytes 52
  137.9 3.3 %copy-start.66 = (f32[4]{0:T(128)S(1)}, f32[4]{0:T(128)}, u32[]{:S(2)}) copy-start(f32[4]{0:T(128)} %get-tuple-element.28) | copy-start | bytes 52
  138.9 2.3 %copy-start.5 = (f32[128,1024]{1,0:T(8,128)S(1)}, f32[128,1024]{1,0:T(8,128)}, u32[]{:S(2)}) copy-start(f32[128,1024]{1,0:T(8,128)} %copy.271) | copy-start | bytes 1572868
  (12 other events, 15.6 us)
